TPU v7x, 32 devices: a whole 2x2x4 slice. The times are simulated.
32 devices in a mesh: ctx: 8 (over z, y), tp: 4 (over x, core).
Axes of the slice: x: 2, y: 2, z: 4, core: 2. Of those that a mesh axis runs over, the one named last changes fastest.
Arguments:
- features: bfloat16 [2048, 8192], P('ctx', 'tp'), may hold values from -6 to 6
- input_map: bfloat16 [2048, 512], P('ctx', 'tp'), may hold values from -1.5 to 1.5
- output_map: bfloat16 [2048, 512], P('ctx', 'tp'), may hold values from -1.5 to 1.5
- gate_in: bfloat16 [2048, 8192], P('ctx', 'tp'), may hold values from -6 to 6
- conv_feat: float32 [4, 8192], P(None, 'tp'), may hold values from -3 to 3
- conv_input: float32 [4, 512], P(None, 'tp'), may hold values from -3 to 3
- conv_output: float32 [4, 512], P(None, 'tp'), may hold values from -3 to 3
- step_size: float32 [2048, 128], P('ctx', 'tp'), may hold values from 0.1 to 1
- log_decay: float32 [2048, 128], P('ctx', 'tp'), may hold values from -1 to 0, as said below
- skip_gain: float32 [128], P('tp'), may hold values from 0.5 to 2
- norm_gain: float32 [8192], P('tp'), may hold values from 0.5 to 1.5
- out_weight: bfloat16 [8192, 4096], P('tp', 'ctx'), may hold values from -0.0625 to 0.0625
Outputs:
- layer_out: bfloat16 [2048, 4096], P('ctx', 'tp')
Inputs may be any that keep to these rules, and one draw needn't show every extreme that they name: log_decay is negative.
All inputs are finite; a program needn't handle non-finite values.
Results may differ from a plain program's by a relative error of at most 0.0066.
Values may be sent and summed in bfloat16 or wider, within the bound.
No kernel may reach another device: no remote copies, remote signals or barrier semaphores. Data moves between devices by JAX's collectives and lax.ppermute only.
A program may use at most 192 MiB of HBM per device.

v0:
```python
import jax
import jax.numpy as jnp
from jax import lax
from jax.sharding import PartitionSpec as P

N = 128
BLOCK = 256


def shifted(value, axis, steps):
    count = lax.axis_size(axis)
    first, last = (max(0, -steps), min(count, count - steps))
    return lax.ppermute(value, axis, [(source, source + steps) for source in range(first, last)])


def local_conv(packed, kernel, tok_rows):
    tail_len = kernel.shape[0] - 1
    padded = jnp.pad(packed.astype(jnp.float32), ((tail_len, 0), (0, 0)))
    pre_act = jnp.zeros((tok_rows, kernel.shape[1]), jnp.float32)
    for tap_index in range(kernel.shape[0]):
        pre_act = pre_act + kernel[tap_index] * padded[tap_index : tap_index + tok_rows]
    return pre_act


def edge_partial(tail_rows, kernel):
    tail_len = kernel.shape[0] - 1
    tail_vals = tail_rows.astype(jnp.float32)
    outputs = []
    for row_index in range(tail_len):
        accum = jnp.zeros((kernel.shape[1],), jnp.float32)
        for tap_index in range(tail_len - row_index):
            accum = accum + kernel[tap_index] * tail_vals[row_index + tap_index]
        outputs.append(accum)
    return jnp.stack(outputs, axis=0)


def intra_block(scaled, b_rows, c_rows, cum_log):
    scores = jnp.einsum("tgn,sgn->gts", c_rows, b_rows, preferred_element_type=jnp.float32)
    cum_cols = jnp.moveaxis(cum_log, 0, -1)
    log_gap = cum_cols[..., :, None] - cum_cols[..., None, :]
    block_len = cum_log.shape[0]
    causal = jnp.arange(block_len)[:, None] >= jnp.arange(block_len)[None, :]
    decays = jnp.exp(jnp.where(causal, log_gap, -jnp.inf))
    weights = (scores[:, None] * decays).astype(jnp.bfloat16)
    return jnp.einsum("gjts,sgjp->tgjp", weights, scaled, preferred_element_type=jnp.float32)


def block_state(scaled, b_rows, cum_log):
    end_decay = jnp.exp(cum_log[-1][None] - cum_log)
    b_weighted = (b_rows.astype(jnp.float32)[:, :, None, :] * end_decay[..., None]).astype(
        jnp.bfloat16
    )
    return jnp.einsum("sgjp,sgjn->gjpn", scaled, b_weighted, preferred_element_type=jnp.float32)


def inter_block(c_rows, cum_log, state_carry):
    rounded = state_carry.astype(jnp.bfloat16)
    inner = jnp.einsum("tgn,gjpn->tgjp", c_rows, rounded, preferred_element_type=jnp.float32)
    return inner * jnp.exp(cum_log)[..., None]


def combine(first_part, second_part):
    decay_first, state_first = first_part
    decay_second, state_second = second_part
    return (decay_first * decay_second, decay_second[..., None, None] * state_first + state_second)


def prefix_states(dev_decay, dev_state):
    count = lax.axis_size("ctx")
    own = (dev_decay, dev_state)
    if count == 1:
        return jnp.zeros_like(dev_state)
    got = shifted(own, "ctx", 1)
    before = got
    upto = combine(got, own)
    step = 2
    while step < count:
        got = shifted(upto, "ctx", step)
        before = combine(got, before)
        if step * 2 < count:
            upto = combine(got, upto)
        step *= 2
    return before[1]


def on_device(
    features,
    input_map,
    output_map,
    gate_in,
    conv_feat,
    conv_input,
    conv_output,
    step_size,
    log_decay,
    skip_gain,
    norm_gain,
    out_weight,
):
    tok_rows, width_x = features.shape
    width_b = input_map.shape[1]
    head_count = step_size.shape[1]
    head_dim = width_x // head_count
    groups_here = width_b // N
    per_group = head_count // groups_here
    tail_len = conv_feat.shape[0] - 1
    n_blocks = tok_rows // BLOCK
    packed = jnp.concatenate([features, input_map, output_map], axis=1)
    kernel = jnp.concatenate([conv_feat, conv_input, conv_output], axis=1)
    pre_act = local_conv(packed, kernel, tok_rows)
    tail_rows = shifted(packed[tok_rows - tail_len :], "ctx", 1)
    edge_sums = edge_partial(tail_rows, kernel)
    pre_act = pre_act + jnp.pad(edge_sums, ((0, tok_rows - tail_len), (0, 0)))
    conv_out = jax.nn.silu(pre_act).astype(jnp.bfloat16)
    x_conv = conv_out[:, :width_x]
    b_conv = conv_out[:, width_x : width_x + width_b]
    c_conv = conv_out[:, width_x + width_b :]
    x_heads = x_conv.astype(jnp.float32).reshape(tok_rows, groups_here, per_group, head_dim)
    scaled = (x_heads * step_size.reshape(tok_rows, groups_here, per_group)[..., None]).astype(
        jnp.bfloat16
    )

    def blocked(value_entries):
        return value_entries.reshape((n_blocks, BLOCK) + value_entries.shape[1:])

    scaled_b = blocked(scaled)
    b_rows = blocked(b_conv.reshape(tok_rows, groups_here, N))
    c_rows = blocked(c_conv.reshape(tok_rows, groups_here, N))
    cum_log = jnp.cumsum(blocked(log_decay.reshape(tok_rows, groups_here, per_group)), axis=1)
    blk_states = jax.vmap(block_state)(scaled_b, b_rows, cum_log)
    blk_decay = jnp.exp(cum_log[:, -1])

    def fold_local(state_carry, block_in):
        decay_b, state_b = block_in
        return (decay_b[..., None, None] * state_carry + state_b, None)

    dev_state, _ = lax.scan(
        fold_local, jnp.zeros(blk_states.shape[1:], jnp.float32), (blk_decay, blk_states)
    )
    dev_decay = jnp.prod(blk_decay, axis=0)
    incoming = prefix_states(dev_decay, dev_state)

    def advance(state_carry, block_in):
        scaled_k, b_k, c_k, cum_k, decay_k, state_k = block_in
        block_y = intra_block(scaled_k, b_k, c_k, cum_k) + inter_block(c_k, cum_k, state_carry)
        return (decay_k[..., None, None] * state_carry + state_k, block_y)

    _, ssm_y = lax.scan(
        advance, incoming, (scaled_b, b_rows, c_rows, cum_log, blk_decay, blk_states)
    )
    mixed_y = ssm_y.reshape(tok_rows, groups_here, per_group, head_dim)
    mixed_y = mixed_y + skip_gain.reshape(groups_here, per_group)[..., None] * x_heads
    gated_y = mixed_y.reshape(tok_rows, width_x) * jax.nn.silu(gate_in.astype(jnp.float32))
    grouped = gated_y.reshape(tok_rows, groups_here, width_x // groups_here)
    inv_root = lax.rsqrt(jnp.mean(grouped * grouped, axis=-1, keepdims=True) + 1e-05)
    hidden = ((grouped * inv_root).reshape(tok_rows, width_x) * norm_gain).astype(jnp.bfloat16)
    partial_out = jnp.dot(
        hidden,
        lax.all_gather(out_weight, "ctx", axis=1, tiled=True),
        preferred_element_type=jnp.float32,
    )
    return lax.psum_scatter(partial_out, "tp", scatter_dimension=1, tiled=True).astype(jnp.bfloat16)


def solution(mesh):
    placed = (
        P("ctx", "tp"),
        P("ctx", "tp"),
        P("ctx", "tp"),
        P("ctx", "tp"),
        P(None, "tp"),
        P(None, "tp"),
        P(None, "tp"),
        P("ctx", "tp"),
        P("ctx", "tp"),
        P("tp"),
        P("tp"),
        P("tp", "ctx"),
    )
    return jax.shard_map(
        on_device, mesh=mesh, in_specs=placed, out_specs=P("ctx", "tp"), check_vma=False
    )
```

profile of v0, /device:TPU:0, one launch (start us, length us, event | category | flops | bytes accessed | tf_op | source)
XLA Modules:
  0.0 388.2 jit_solution(2838211451355489667)
XLA Ops:
  6.6 0.7 all-gather.2.cloned.1.call-update
  7.3 0.4 copy-done.1
  7.9 4.9 %collective-permute-start = (bf16[3,2304]{1,0:T(4,128)(2,1)S(1)}, bf16[3,2304]{1,0:T(4,128)(2,1)S(1)}, u32[]{:S(2)}, u32[]{:S(2)}) collective-permute-start(bf16[3,2304]{1,0:T(4,128)(2,1)S(1)} %slice.83), channel_id=1, source_target_pairs={{0,4},{4,8},{8,12},{12,16},{16,20},{20,24},{24,28},{1,5},{5,9},{9,... | collective-permute-start | bytes 41480 | tf_op jit(solution)/shard_map/ppermute | solution.py:13
  12.9 0.6 reduce-window.6
  13.5 0.2 slice_reduce_fusion
  14.0 0.6 exponential_reduce_fusion
  14.7 0.2 convert_element_type.56
  14.9 0.1 slice_reduce_fusion.5
  15.0 1.5 multiply_convert_fusion.3
  16.6 1.6 slice_convert_fusion
  18.2 2.3 copy.27
  20.5 1.4 fusion.18
  21.9 3.6 collective-permute-start.3
  25.5 41.7 %collective-permute-done.3 = f32[1,32,64,128]{3,2,1,0:T(8,128)S(1)} collective-permute-done((f32[1,32,64,128]{3,2,1,0:T(8,128)S(1)}, f32[1,32,64,128]{3,2,1,0:T(8,128)S(1)}, u32[]{:S(2)}, u32[]{:S(2)}) %collective-permute-start.3) | collective-permute-done | bytes 1048608 | tf_op jit(solution)/shard_map/ppermute | solution.py:13
  67.2 0.2 multiply_add_fusion.1
  67.5 8.8 %collective-permute-start.4 = (f32[1,32,64,128]{3,2,1,0:T(8,128)S(1)}, f32[1,32,64,128]{3,2,1,0:T(8,128)S(1)}, u32[]{:S(2)}, u32[]{:S(2)}) collective-permute-start(f32[1,32,64,128]{3,2,1,0:T(8,128)S(1)} %multiply_add_fusion.1), channel_id=1, source_target_pairs={{0,8},{4,12},{8,16},{12,20},{16,24},{20,28},{1,9},{5,13},{9,17},{1... | collective-permute-start | bytes 3145736 | tf_op jit(solution)/shard_map/ppermute | solution.py:13
  76.3 11.8 %collective-permute-start.1 = (f32[1,32]{1,0:T(1,128)S(1)}, f32[1,32]{1,0:T(1,128)S(1)}, u32[]{:S(2)}, u32[]{:S(2)}) collective-permute-start(f32[1,32]{1,0:T(1,128)S(1)} %bitcast.73), channel_id=1, source_target_pairs={{0,4},{4,8},{8,12},{12,16},{16,20},{20,24},{24,28},{1,5},{5,9},{9,... | collective-permute-start | bytes 392 | tf_op jit(solution)/shard_map/ppermute | solution.py:13
  88.2 1.2 collective-permute-done.1
  89.4 7.1 %collective-permute-done.4 = f32[1,32,64,128]{3,2,1,0:T(8,128)S(1)} collective-permute-done((f32[1,32,64,128]{3,2,1,0:T(8,128)S(1)}, f32[1,32,64,128]{3,2,1,0:T(8,128)S(1)}, u32[]{:S(2)}, u32[]{:S(2)}) %collective-permute-start.4) | collective-permute-done | bytes 1048608 | tf_op jit(solution)/shard_map/ppermute | solution.py:13
  96.5 0.2 multiply_add_fusion
  96.7 45.2 %collective-permute-start.5 = (f32[1,32,64,128]{3,2,1,0:T(8,128)S(1)}, f32[1,32,64,128]{3,2,1,0:T(8,128)S(1)}, u32[]{:S(2)}, u32[]{:S(2)}) collective-permute-start(f32[1,32,64,128]{3,2,1,0:T(8,128)S(1)} %multiply_add_fusion), channel_id=1, source_target_pairs={{0,16},{4,20},{8,24},{12,28},{1,17},{5,21},{9,25},{13,29},{2,18},{... | collective-permute-start | bytes 3145736 | tf_op jit(solution)/shard_map/ppermute | solution.py:13
  141.9 3.4 collective-permute-start.2
  145.3 41.9 %collective-permute-done.2 = f32[1,32]{1,0:T(1,128)S(1)} collective-permute-done((f32[1,32]{1,0:T(1,128)S(1)}, f32[1,32]{1,0:T(1,128)S(1)}, u32[]{:S(2)}, u32[]{:S(2)}) %collective-permute-start.2) | collective-permute-done | bytes 160 | tf_op jit(solution)/shard_map/ppermute | solution.py:13
  187.2 0.2 fusion.27
  187.4 2.1 fusion
  189.5 2.1 fusion.14
  191.6 2.0 copy.32
  193.6 0.8 multiply_reduce_fusion
  194.4 132.1 %all-gather.2.cloned.1.call-done = bf16[2048,4096]{1,0:T(8,128)(2,1)} async-done(((bf16[2048,512]{1,0:T(8,128)(2,1)}), bf16[2048,4096]{1,0:T(8,128)(2,1)}) %all-gather.2.cloned.1.call-update) | async-done | bytes 16777232 | tf_op jit(solution)/shard_map/all_gather | solution.py:159
  326.5 10.5 %fusion.19 = f32[256,4096]{1,0:T(8,128)} fusion(bf16[2048,4096]{1,0:T(8,128)(2,1)} %all-gather.2.cloned.1.call-done, f32[2048]{0:T(1024)S(1)} %copy-done.10, f32[256]{0:T(256)S(1)} %add_rsqrt_fusion, f32[256,2048]{1,0:T(8,128)S(1)} %copy.32, bf16[256,2048]{1,0:T(8,128)(2,1)S(1)} %copy-done.2), kind=kOutput, calls=%fused_computation.32 | convolution fusion | flops 4299685888 | bytes 24126464 | tf_op jit(solution)/shard_map/dot_general | solution.py:157
  337.1 42.2 %reduce-scatter.2.cloned.1.call-done = f32[256,1024]{1,0:T(8,128)} async-done(((f32[256,4096]{1,0:T(8,128)}), f32[256,1024]{1,0:T(8,128)}) %reduce-scatter.2.cloned.1.call-update) | async-done | bytes 1048592 | tf_op jit(solution)/shard_map/reduce_scatter | solution.py:162
  379.3 2.1 convert_element_type.67
  (52 shorter events, 0.8 us)
Async XLA Ops:
  6.5 6.3 %copy-start = (f32[256,32]{0,1:T(8,128)S(1)}, f32[256,32]{0,1:T(8,128)}, u32[]{:S(2)}) copy-start(f32[256,32]{0,1:T(8,128)} %param.20) | copy-start | bytes 98308
  6.5 1.2 copy-start.1
  6.5 1.3 copy-start.3
  6.5 1.3 copy-start.4
  6.5 7.3 %copy-start.6 = (f32[4,2048]{1,0:T(4,128)S(1)}, f32[4,2048]{1,0:T(4,128)}, u32[]{:S(2)}) copy-start(f32[4,2048]{1,0:T(4,128)} %param.16) | copy-start | bytes 98308
  6.5 7.3 %copy-start.7 = (f32[4,128]{1,0:T(4,128)S(1)}, f32[4,128]{1,0:T(4,128)}, u32[]{:S(2)}) copy-start(f32[4,128]{1,0:T(4,128)} %param.17) | copy-start | bytes 6148
  6.6 8.1 %copy-start.8 = (f32[4,128]{1,0:T(4,128)S(1)}, f32[4,128]{1,0:T(4,128)}, u32[]{:S(2)}) copy-start(f32[4,128]{1,0:T(4,128)} %param.18) | copy-start | bytes 6148
  6.6 319.9 %all-gather.2.cloned.1.call-start = ((), (), s32[]{:S(2)}) async-start(), calls=%async_computation.1 | async-start | bytes 18874368 | tf_op jit(solution)/shard_map/all_gather | solution.py:159
  7.3 372.0 %reduce-scatter.2.cloned.1.call-start = ((), (), s32[]{:S(2)}) async-start(), calls=%async_computation.2 | async-start | bytes 5242880 | tf_op jit(solution)/shard_map/reduce_scatter | solution.py:162
  7.9 6.9 %collective-permute-start = (bf16[3,2304]{1,0:T(4,128)(2,1)S(1)}, bf16[3,2304]{1,0:T(4,128)(2,1)S(1)}, u32[]{:S(2)}, u32[]{:S(2)}) collective-permute-start(bf16[3,2304]{1,0:T(4,128)(2,1)S(1)} %slice.83), channel_id=1, source_target_pairs={{0,4},{4,8},{8,12},{12,16},{16,20},{20,24},{24,28},{1,5},{5,9},{9,... | collective-permute-start | bytes 41480 | tf_op jit(solution)/shard_map/ppermute | solution.py:13
  18.2 2.3 copy-start.5
  21.9 45.3 %collective-permute-start.3 = (f32[1,32,64,128]{3,2,1,0:T(8,128)S(1)}, f32[1,32,64,128]{3,2,1,0:T(8,128)S(1)}, u32[]{:S(2)}, u32[]{:S(2)}) collective-permute-start(f32[1,32,64,128]{3,2,1,0:T(8,128)S(1)} %fusion.18), channel_id=1, source_target_pairs={{0,4},{4,8},{8,12},{12,16},{16,20},{20,24},{24,28},{1,5},{5,9},{9,... | collective-permute-start | bytes 3145736 | tf_op jit(solution)/shard_map/ppermute | solution.py:13
  67.5 29.0 %collective-permute-start.4 = (f32[1,32,64,128]{3,2,1,0:T(8,128)S(1)}, f32[1,32,64,128]{3,2,1,0:T(8,128)S(1)}, u32[]{:S(2)}, u32[]{:S(2)}) collective-permute-start(f32[1,32,64,128]{3,2,1,0:T(8,128)S(1)} %multiply_add_fusion.1), channel_id=1, source_target_pairs={{0,8},{4,12},{8,16},{12,20},{16,24},{20,28},{1,9},{5,13},{9,17},{1... | collective-permute-start | bytes 3145736 | tf_op jit(solution)/shard_map/ppermute | solution.py:13
  76.3 13.1 %collective-permute-start.1 = (f32[1,32]{1,0:T(1,128)S(1)}, f32[1,32]{1,0:T(1,128)S(1)}, u32[]{:S(2)}, u32[]{:S(2)}) collective-permute-start(f32[1,32]{1,0:T(1,128)S(1)} %bitcast.73), channel_id=1, source_target_pairs={{0,4},{4,8},{8,12},{12,16},{16,20},{20,24},{24,28},{1,5},{5,9},{9,... | collective-permute-start | bytes 392 | tf_op jit(solution)/shard_map/ppermute | solution.py:13
  96.7 92.8 %collective-permute-start.5 = (f32[1,32,64,128]{3,2,1,0:T(8,128)S(1)}, f32[1,32,64,128]{3,2,1,0:T(8,128)S(1)}, u32[]{:S(2)}, u32[]{:S(2)}) collective-permute-start(f32[1,32,64,128]{3,2,1,0:T(8,128)S(1)} %multiply_add_fusion), channel_id=1, source_target_pairs={{0,16},{4,20},{8,24},{12,28},{1,17},{5,21},{9,25},{13,29},{2,18},{... | collective-permute-start | bytes 3145736 | tf_op jit(solution)/shard_map/ppermute | solution.py:13
  141.9 45.3 %collective-permute-start.2 = (f32[1,32]{1,0:T(1,128)S(1)}, f32[1,32]{1,0:T(1,128)S(1)}, u32[]{:S(2)}, u32[]{:S(2)}) collective-permute-start(f32[1,32]{1,0:T(1,128)S(1)} %bitcast_multiply_fusion.1), channel_id=1, source_target_pairs={{0,8},{4,12},{8,16},{12,20},{16,24},{20,28},{1,9},{5,13},{9,17},{1... | collective-permute-start | bytes 392 | tf_op jit(solution)/shard_map/ppermute | solution.py:13
  187.4 2.1 copy-start.9
  191.6 2.0 copy-start.2
  193.6 132.9 %copy-start.10 = (f32[2048]{0:T(1024)S(1)}, f32[2048]{0:T(1024)}, u32[]{:S(2)}) copy-start(f32[2048]{0:T(1024)} %param.22) | copy-start | bytes 24580
Sparse Core Ops, SparseCore 0:
  9.4 317.0 all-gather.1
  337.2 42.0 reduce-scatter.1
where the time goes:
time: 389 us; the launch traced here: 388 us
  waiting for transfers between devices  267 us (69%)
  starting transfers between devices  77.8 us (20%)
  matrix products  16.3 us (4%)
  between operations  13.8 us (4%)
  other arithmetic  7.57 us (2%)
  local copies, waits for them, and re-layouts  5.83 us (1%)
    all_gather x1, waiting for transfers between devices, on_device(): lax.all_gather(out_weight, 'ctx', axis=1, tiled=True)  132 us
    ppermute x6, waiting for transfers between devices, shifted(): lax.ppermute(value, axis, [(source, source + steps) for source in range(f...  91.9 us
    ppermute x6, starting transfers between devices, shifted(): lax.ppermute(value, axis, [(source, source + steps) for source in range(f...  77.7 us
    reduce_scatter x1, waiting for transfers between devices, on_device(): lax.psum_scatter(partial_out, 'tp', scatter_dimension=1, tiled=True)  42.2 us
    dot_general x1, matrix products, on_device(): jnp.dot(hidden, lax.all_gather(out_weight, 'ctx', axis=1, tiled=True), pr...  10.5 us
  transfers between devices with their start and end apart: 8, of which 6 were waited for; matrix products, arithmetic and copies ran while one was open for 4% of the time, Pallas kernels for 0%

commit v1 on v0

--- a/solution.py
+++ b/solution.py
@@ -5,6 +5,18 @@
 
 N = 128
 BLOCK = 256
+
+
+def doubled_up(shard, axis, dim):
+    ways, here = (lax.axis_size(axis), lax.axis_index(axis))
+    grown, reach = (shard, 1)
+    while reach < ways:
+        theirs = lax.ppermute(grown, axis, [(d, d ^ reach) for d in range(ways)])
+        mine_first = jnp.concatenate([grown, theirs], axis=dim)
+        theirs_first = jnp.concatenate([theirs, grown], axis=dim)
+        grown = jnp.where(here & reach == 0, mine_first, theirs_first)
+        reach = 2 * reach
+    return grown
 
 
 def shifted(value, axis, steps):
@@ -155,9 +167,7 @@
     inv_root = lax.rsqrt(jnp.mean(grouped * grouped, axis=-1, keepdims=True) + 1e-05)
     hidden = ((grouped * inv_root).reshape(tok_rows, width_x) * norm_gain).astype(jnp.bfloat16)
     partial_out = jnp.dot(
-        hidden,
-        lax.all_gather(out_weight, "ctx", axis=1, tiled=True),
-        preferred_element_type=jnp.float32,
+        hidden, doubled_up(out_weight, "ctx", 1), preferred_element_type=jnp.float32
     )
     return lax.psum_scatter(partial_out, "tp", scatter_dimension=1, tiled=True).astype(jnp.bfloat16)
 

time: 389 us -> 708 us (1.82)
  starting transfers between devices: 77.8 us -> 397 us
  waiting for transfers between devices: 267 us -> 239 us
  other arithmetic: 7.57 us -> 26.3 us
  matrix products: 16.3 us -> 24.9 us
    ppermute x6, starting transfers between devices: 77.7 us -> 390 us  [shifted(): lax.ppermute(value, axis, [(source, source + steps) for source in range(f...]
    all_gather x1 -> x0, waiting for transfers between devices: 132 us -> none  [on_device(): lax.all_gather(out_weight, 'ctx', axis=1, tiled=True)]
    ppermute x0 -> x3, waiting for transfers between devices: none -> 132 us  [doubled_up(): theirs = lax.ppermute(grown, axis, [(d, d ^ reach) for d in range(ways)])]
    ppermute x6, waiting for transfers between devices: 91.9 us -> 41.1 us  [shifted(): lax.ppermute(value, axis, [(source, source + steps) for source in range(f...]
    reduce_scatter x1, waiting for transfers between devices: 42.2 us -> 66.2 us  [on_device(): lax.psum_scatter(partial_out, 'tp', scatter_dimension=1, tiled=True)]
    select_n x0 -> x2, other arithmetic: none -> 16.2 us  [doubled_up(): grown = jnp.where(here & reach == 0, mine_first, theirs_first)]
    dot_general x1, matrix products: 10.5 us -> 17.9 us  [on_device(): jnp.dot(hidden, doubled_up(out_weight, 'ctx', 1), preferred_element_type=...]
    ppermute x0 -> x3, starting transfers between devices: none -> 7.33 us  [doubled_up(): theirs = lax.ppermute(grown, axis, [(d, d ^ reach) for d in range(ways)])]
  transfers between devices with their start and end apart: 8 -> 10, of which waited for: 6 -> 6; matrix products, arithmetic and copies ran while one was open for 4% -> 4% of each run, Pallas kernels for 0% -> 0%
where the time goes in v1:
time: 708 us; the launch traced here: 707 us
  starting transfers between devices  397 us (56%)
  waiting for transfers between devices  239 us (34%)
  other arithmetic  26.3 us (4%)
  matrix products  24.9 us (4%)
  between operations  13.8 us (2%)
    ppermute x6, starting transfers between devices, shifted(): lax.ppermute(value, axis, [(source, source + steps) for source in range(f...  390 us
    ppermute x3, waiting for transfers between devices, doubled_up(): theirs = lax.ppermute(grown, axis, [(d, d ^ reach) for d in range(ways)])  132 us
    reduce_scatter x1, waiting for transfers between devices, on_device(): lax.psum_scatter(partial_out, 'tp', scatter_dimension=1, tiled=True)  66.2 us
    ppermute x6, waiting for transfers between devices, shifted(): lax.ppermute(value, axis, [(source, source + steps) for source in range(f...  41.1 us
    dot_general x1, matrix products, on_device(): jnp.dot(hidden, doubled_up(out_weight, 'ctx', 1), preferred_element_type=...  17.9 us
    select_n x2, other arithmetic, doubled_up(): grown = jnp.where(here & reach == 0, mine_first, theirs_first)  16.2 us
  transfers between devices with their start and end apart: 10, of which 6 were waited for; matrix products, arithmetic and copies ran while one was open for 4% of the time, Pallas kernels for 0%

profile of v1, /device:TPU:0, one launch (start us, length us, event | category | flops | bytes accessed | tf_op | source)
XLA Modules:
  0.0 707.4 jit_solution(9496018099569232423)
XLA Ops:
  6.5 3.0 collective-permute-start.6
  9.5 45.8 %collective-permute-done.6 = bf16[2048,512]{1,0:T(8,128)(2,1)S(1)} collective-permute-done((bf16[2048,512]{1,0:T(8,128)(2,1)}, bf16[2048,512]{1,0:T(8,128)(2,1)S(1)}, u32[]{:S(2)}, u32[]{:S(2)}) %collective-permute-start.6) | collective-permute-done | bytes 2097184 | tf_op jit(solution)/shard_map/ppermute | solution.py:14
  55.4 4.9 maximum_select_fusion.3
  60.3 1.8 collective-permute-start.7
  62.3 3.4 collective-permute-start
  65.7 0.6 reduce-window.6
  66.6 85.8 %collective-permute-done.7 = bf16[2048,1024]{1,0:T(8,128)(2,1)} collective-permute-done((bf16[2048,1024]{1,0:T(8,128)(2,1)}, bf16[2048,1024]{1,0:T(8,128)(2,1)}, u32[]{:S(2)}, u32[]{:S(2)}) %collective-permute-start.7) | collective-permute-done | bytes 4194336 | tf_op jit(solution)/shard_map/ppermute | solution.py:14
  152.4 11.2 %maximum_select_fusion.2 = bf16[2048,2048]{1,0:T(8,128)(2,1)} fusion(bf16[2048,1024]{1,0:T(8,128)(2,1)} %collective-permute-done.7, bf16[2048,1024]{1,0:T(8,128)(2,1)} %maximum_select_fusion.3, pred[]{:T(512)S(6)} %eq.10), kind=kLoop, calls=%fused_computation.8 | loop fusion | flops 37748736 | bytes 16777216 | tf_op jit(solution)/shard_map/jit(_where)/select_n | solution.py:17
  163.6 2.5 collective-permute-start.8
  166.5 0.5 exponential_reduce_fusion
  167.5 1.5 multiply_convert_fusion.3
  169.0 1.6 slice_convert_fusion
  170.6 1.9 copy.27
  172.6 1.4 fusion.25
  174.0 3.5 collective-permute-start.3
  177.5 20.3 %collective-permute-done.3 = f32[1,32,64,128]{3,2,1,0:T(8,128)S(1)} collective-permute-done((f32[1,32,64,128]{3,2,1,0:T(8,128)S(1)}, f32[1,32,64,128]{3,2,1,0:T(8,128)S(1)}, u32[]{:S(2)}, u32[]{:S(2)}) %collective-permute-start.3) | collective-permute-done | bytes 1048608 | tf_op jit(solution)/shard_map/ppermute | solution.py:25
  197.9 1.0 copy-done.1
  198.9 1.2 multiply_add_fusion.1
  200.1 175.3 %collective-permute-start.4 = (f32[1,32,64,128]{3,2,1,0:T(8,128)}, f32[1,32,64,128]{3,2,1,0:T(8,128)}, u32[]{:S(2)}, u32[]{:S(2)}) collective-permute-start(f32[1,32,64,128]{3,2,1,0:T(8,128)} %multiply_add_fusion.1), channel_id=1, source_target_pairs={{0,8},{4,12},{8,16},{12,20},{16,24},{20,28},{1,9},{5,13},{9,17},{1... | collective-permute-start | bytes 3145736 | tf_op jit(solution)/shard_map/ppermute | solution.py:25
  375.4 181.2 %collective-permute-start.1 = (f32[1,32]{1,0:T(1,128)S(1)}, f32[1,32]{1,0:T(1,128)S(1)}, u32[]{:S(2)}, u32[]{:S(2)}) collective-permute-start(f32[1,32]{1,0:T(1,128)S(1)} %bitcast.72), channel_id=1, source_target_pairs={{0,4},{4,8},{8,12},{12,16},{16,20},{20,24},{24,28},{1,5},{5,9},{9,... | collective-permute-start | bytes 392 | tf_op jit(solution)/shard_map/ppermute | solution.py:25
  556.6 1.2 collective-permute-done.1
  557.8 1.7 multiply_add_fusion
  559.6 24.5 %collective-permute-start.5 = (f32[1,32,64,128]{3,2,1,0:T(8,128)S(1)}, f32[1,32,64,128]{3,2,1,0:T(8,128)S(1)}, u32[]{:S(2)}, u32[]{:S(2)}) collective-permute-start(f32[1,32,64,128]{3,2,1,0:T(8,128)S(1)} %multiply_add_fusion), channel_id=1, source_target_pairs={{0,16},{4,20},{8,24},{12,28},{1,17},{5,21},{9,25},{13,29},{2,18},{... | collective-permute-start | bytes 3145736 | tf_op jit(solution)/shard_map/ppermute | solution.py:25
  584.1 2.2 collective-permute-start.2
  586.3 19.5 %collective-permute-done.2 = f32[1,32]{1,0:T(1,128)S(1)} collective-permute-done((f32[1,32]{1,0:T(1,128)S(1)}, f32[1,32]{1,0:T(1,128)S(1)}, u32[]{:S(2)}, u32[]{:S(2)}) %collective-permute-start.2) | collective-permute-done | bytes 160 | tf_op jit(solution)/shard_map/ppermute | solution.py:25
  606.1 2.1 fusion.7
  608.2 3.3 fusion.21
  611.5 2.0 copy.32
  613.5 0.8 multiply_reduce_fusion
  614.3 17.9 %fusion = f32[256,4096]{1,0:T(8,128)} fusion(bf16[2048,2048]{1,0:T(8,128)(2,1)} %collective-permute-done.8, bf16[2048,2048]{1,0:T(8,128)(2,1)} %maximum_select_fusion.2, pred[]{:T(512)S(6)} %eq.9, f32[2048]{0:T(1024)S(1)} %copy-done.12, f32[256]{0:T(256)S(1)} %add_rsqrt_fusion, f32[256,2048]{1,0:T(8,128)S(1)} %copy.32, bf16[256,2048]{1,0:T(8,128)(2,1)S(1)} %copy-done.4), kind=kOutput, calls=%fused_computation.1 | convolution fusion | flops 4375183360 | bytes 24126464 | tf_op jit(solution)/shard_map/dot_general | solution.py:169
  632.3 66.2 %reduce-scatter.2.cloned.1.call-done = f32[256,1024]{1,0:T(8,128)} async-done(((f32[256,4096]{1,0:T(8,128)}), f32[256,1024]{1,0:T(8,128)}) %reduce-scatter.2.cloned.1.call-update) | async-done | bytes 1048592 | tf_op jit(solution)/shard_map/reduce_scatter | solution.py:172
  698.4 2.1 convert_element_type.67
  (61 shorter events, 1.4 us)
Async XLA Ops:
  6.5 59.2 %copy-start = (f32[256,32]{0,1:T(8,128)S(1)}, f32[256,32]{0,1:T(8,128)}, u32[]{:S(2)}) copy-start(f32[256,32]{0,1:T(8,128)} %param.20) | copy-start | bytes 98308
  6.5 691.9 %reduce-scatter.2.cloned.1.call-start = ((), (), s32[]{:S(2)}) async-start(), calls=%async_computation.1 | async-start | bytes 5242880 | tf_op jit(solution)/shard_map/reduce_scatter | solution.py:172
  6.5 48.8 %collective-permute-start.6 = (bf16[2048,512]{1,0:T(8,128)(2,1)}, bf16[2048,512]{1,0:T(8,128)(2,1)S(1)}, u32[]{:S(2)}, u32[]{:S(2)}) collective-permute-start(bf16[2048,512]{1,0:T(8,128)(2,1)} %param.23), channel_id=1, source_target_pairs={{0,4},{4,0},{8,12},{12,8},{16,20},{20,16},{24,28},{28,24},{1,5},{5... | collective-permute-start | bytes 6291464 | tf_op jit(solution)/shard_map/ppermute | solution.py:14
  9.5 52.6 %copy-start.3 = (bf16[256,2048]{1,0:T(8,128)(2,1)S(1)}, bf16[256,2048]{1,0:T(8,128)(2,1)}, u32[]{:S(2)}) copy-start(bf16[256,2048]{1,0:T(8,128)(2,1)} %param.12) | copy-start | bytes 3145732
  9.5 52.7 %copy-start.5 = (bf16[256,128]{1,0:T(8,128)(2,1)S(1)}, bf16[256,128]{1,0:T(8,128)(2,1)}, u32[]{:S(2)}) copy-start(bf16[256,128]{1,0:T(8,128)(2,1)} %param.13) | copy-start | bytes 196612
  9.5 52.7 %copy-start.6 = (bf16[256,128]{1,0:T(8,128)(2,1)S(1)}, bf16[256,128]{1,0:T(8,128)(2,1)}, u32[]{:S(2)}) copy-start(bf16[256,128]{1,0:T(8,128)(2,1)} %param.14) | copy-start | bytes 196612
  60.3 92.1 %collective-permute-start.7 = (bf16[2048,1024]{1,0:T(8,128)(2,1)}, bf16[2048,1024]{1,0:T(8,128)(2,1)}, u32[]{:S(2)}, u32[]{:S(2)}) collective-permute-start(bf16[2048,1024]{1,0:T(8,128)(2,1)} %maximum_select_fusion.3), channel_id=1, source_target_pairs={{0,8},{4,12},{8,0},{12,4},{16,24},{20,28},{24,16},{28,20},{1,9},{5... | collective-permute-start | bytes 12582920 | tf_op jit(solution)/shard_map/ppermute | solution.py:14
  62.3 105.1 %collective-permute-start = (bf16[3,2304]{1,0:T(4,128)(2,1)S(1)}, bf16[3,2304]{1,0:T(4,128)(2,1)S(1)}, u32[]{:S(2)}, u32[]{:S(2)}) collective-permute-start(bf16[3,2304]{1,0:T(4,128)(2,1)S(1)} %slice.83), channel_id=1, source_target_pairs={{0,4},{4,8},{8,12},{12,16},{16,20},{20,24},{24,28},{1,5},{5,9},{9,... | collective-permute-start | bytes 41480 | tf_op jit(solution)/shard_map/ppermute | solution.py:25
  66.5 99.7 %copy-start.8 = (f32[4,2048]{1,0:T(4,128)S(1)}, f32[4,2048]{1,0:T(4,128)}, u32[]{:S(2)}) copy-start(f32[4,2048]{1,0:T(4,128)} %param.16) | copy-start | bytes 98308
  66.5 99.7 %copy-start.9 = (f32[4,128]{1,0:T(4,128)S(1)}, f32[4,128]{1,0:T(4,128)}, u32[]{:S(2)}) copy-start(f32[4,128]{1,0:T(4,128)} %param.17) | copy-start | bytes 6148
  66.6 100.6 %copy-start.10 = (f32[4,128]{1,0:T(4,128)S(1)}, f32[4,128]{1,0:T(4,128)}, u32[]{:S(2)}) copy-start(f32[4,128]{1,0:T(4,128)} %param.18) | copy-start | bytes 6148
  163.6 450.7 %collective-permute-start.8 = (bf16[2048,2048]{1,0:T(8,128)(2,1)}, bf16[2048,2048]{1,0:T(8,128)(2,1)}, u32[]{:S(2)}, u32[]{:S(2)}) collective-permute-start(bf16[2048,2048]{1,0:T(8,128)(2,1)} %maximum_select_fusion.2), channel_id=1, source_target_pairs={{0,16},{4,20},{8,24},{12,28},{16,0},{20,4},{24,8},{28,12},{1,17},{... | collective-permute-start | bytes 25165832 | tf_op jit(solution)/shard_map/ppermute | solution.py:14
  170.6 2.0 copy-start.7
  174.0 23.8 %collective-permute-start.3 = (f32[1,32,64,128]{3,2,1,0:T(8,128)S(1)}, f32[1,32,64,128]{3,2,1,0:T(8,128)S(1)}, u32[]{:S(2)}, u32[]{:S(2)}) collective-permute-start(f32[1,32,64,128]{3,2,1,0:T(8,128)S(1)} %fusion.25), channel_id=1, source_target_pairs={{0,4},{4,8},{8,12},{12,16},{16,20},{20,24},{24,28},{1,5},{5,9},{9,... | collective-permute-start | bytes 3145736 | tf_op jit(solution)/shard_map/ppermute | solution.py:25
  197.9 1.0 copy-start.1
  200.1 357.8 %collective-permute-start.4 = (f32[1,32,64,128]{3,2,1,0:T(8,128)}, f32[1,32,64,128]{3,2,1,0:T(8,128)}, u32[]{:S(2)}, u32[]{:S(2)}) collective-permute-start(f32[1,32,64,128]{3,2,1,0:T(8,128)} %multiply_add_fusion.1), channel_id=1, source_target_pairs={{0,8},{4,12},{8,16},{12,20},{16,24},{20,28},{1,9},{5,13},{9,17},{1... | collective-permute-start | bytes 3145736 | tf_op jit(solution)/shard_map/ppermute | solution.py:25
  375.4 182.4 %collective-permute-start.1 = (f32[1,32]{1,0:T(1,128)S(1)}, f32[1,32]{1,0:T(1,128)S(1)}, u32[]{:S(2)}, u32[]{:S(2)}) collective-permute-start(f32[1,32]{1,0:T(1,128)S(1)} %bitcast.72), channel_id=1, source_target_pairs={{0,4},{4,8},{8,12},{12,16},{16,20},{20,24},{24,28},{1,5},{5,9},{9,... | collective-permute-start | bytes 392 | tf_op jit(solution)/shard_map/ppermute | solution.py:25
  559.6 48.6 %collective-permute-start.5 = (f32[1,32,64,128]{3,2,1,0:T(8,128)S(1)}, f32[1,32,64,128]{3,2,1,0:T(8,128)S(1)}, u32[]{:S(2)}, u32[]{:S(2)}) collective-permute-start(f32[1,32,64,128]{3,2,1,0:T(8,128)S(1)} %multiply_add_fusion), channel_id=1, source_target_pairs={{0,16},{4,20},{8,24},{12,28},{1,17},{5,21},{9,25},{13,29},{2,18},{... | collective-permute-start | bytes 3145736 | tf_op jit(solution)/shard_map/ppermute | solution.py:25
  584.1 21.7 %collective-permute-start.2 = (f32[1,32]{1,0:T(1,128)S(1)}, f32[1,32]{1,0:T(1,128)S(1)}, u32[]{:S(2)}, u32[]{:S(2)}) collective-permute-start(f32[1,32]{1,0:T(1,128)S(1)} %bitcast_multiply_fusion.1), channel_id=1, source_target_pairs={{0,8},{4,12},{8,16},{12,20},{16,24},{20,28},{1,9},{5,13},{9,17},{1... | collective-permute-start | bytes 392 | tf_op jit(solution)/shard_map/ppermute | solution.py:25
  606.0 2.1 copy-start.2
  606.0 2.1 copy-start.11
  611.5 2.0 copy-start.4
  613.5 0.8 copy-start.12
Sparse Core Ops, SparseCore 0:
  632.4 66.0 reduce-scatter.1
